TPU v7x, 256 devices: a whole 4x4x8 slice. The times are simulated.
256 devices in a mesh: dp: 2 (over core), ctx: 8 (over y, z_lo), feat: 16 (over x, z_hi).
Axes of the slice: x: 4, y: 4, z: 8 (z_hi: 4, z_lo: 2; z = z_hi * 2 + z_lo), core: 2. Of those that a mesh axis runs over, the one named last changes fastest.
Arguments:
- out_grads: bfloat16 [2048, 28672], P(('dp', 'ctx'), 'feat'), may hold values from -6 to 6
- acts: bfloat16 [2048, 8192], P(('dp', 'ctx'), 'feat'), may hold values from -6 to 6
- domain_ids: int32 [2048], P(('dp', 'ctx')), may hold values from 0 to 7
- domain_weights: int32 [8], replicated, may hold values from 1 to 4
Outputs:
- grad_factor: bfloat16 [28672, 28672], P(('dp', 'ctx'), 'feat')
- act_factor: bfloat16 [8192, 8192], P(('dp', 'ctx'), 'feat')
All inputs are finite; a program needn't handle non-finite values.
Results may differ from a plain program's by a relative error of at most 0.003.
Values may be sent and summed in bfloat16 or wider, within the bound.
No kernel may reach another device: no remote copies, remote signals or barrier semaphores. Data moves between devices by JAX's collectives and lax.ppermute only.
A program may use at most 128 MiB of HBM per device.

v0:
```python
import jax
import jax.numpy as jnp
from jax import lax
from jax.sharding import PartitionSpec as P

ROWS = ("dp", "ctx")
PAIR = 2


def token_weights(tok_ids, domain_weights):
    labels = jnp.arange(domain_weights.shape[0], dtype=jnp.int32)
    match = tok_ids[:, None] == labels[None, :]
    return jnp.sum(jnp.where(match, domain_weights[None, :], 0), axis=1).astype(jnp.float32)


def contract_tokens(left, right):
    return lax.dot_general(
        left, right, (((0,), (0,)), ((), ())), preferred_element_type=jnp.float32
    )


def split_row(r, n_ring):
    per_dp = n_ring * PAIR
    return (r // per_dp, r % per_dp // PAIR, r % PAIR)


def token_block(r, p, n_dp, n_ring):
    dp, y, z = split_row(r, n_ring)
    ddp, dy, dz = split_row(p, n_ring)
    return (dp + ddp) % n_dp * n_ring * PAIR + (y + dy) % n_ring * PAIR + (z + dz) % PAIR


def transpose_pairs(n_rows, n_cols, n_dp, n_ring):
    return [
        (token_block(r, c, n_dp, n_ring) * n_cols + r, r * n_cols + c)
        for r in range(n_rows)
        for c in range(n_cols)
    ]


def ctx_shift(n_ring, dy, dz):
    pairs = []
    for y in range(n_ring):
        for z in range(PAIR):
            src = (y + dy) % n_ring * PAIR + (z + dz) % PAIR
            pairs.append((src, y * PAIR + z))
    return pairs


def gather_columns(block, n_dp, n_ring):
    half = block.shape[0]
    near = lax.ppermute(block, "ctx", ctx_shift(n_ring, 0, 1))
    own = jnp.concatenate([block, near], axis=0)
    ahead = lax.ppermute(own, "ctx", ctx_shift(n_ring, 1, 0))
    behind = lax.ppermute(own, "ctx", ctx_shift(n_ring, -1, 0))
    far_a = lax.ppermute(ahead[:half], "ctx", ctx_shift(n_ring, 1, 0))
    far_b = lax.ppermute(behind[half:], "ctx", ctx_shift(n_ring, -1, 0))
    mine = jnp.concatenate([own, ahead, far_a, far_b, behind], axis=0)
    other = lax.ppermute(mine, "dp", [(1, 0), (0, 1)])
    return jnp.concatenate([mine, other], axis=0)


def local(out_grads, acts, domain_ids, domain_weights):
    n_dp = lax.axis_size("dp")
    n_ctx = lax.axis_size("ctx")
    n_rows = n_dp * n_ctx
    n_cols = lax.axis_size("feat")
    n_ring = n_ctx // PAIR
    assert n_rows == n_cols and n_dp == 2 and (n_ring == 4) and (n_ctx % PAIR == 0)
    inv_count = 1.0 / (out_grads.shape[0] * n_rows)
    width_g = out_grads.shape[1]
    both = jnp.concatenate([out_grads, acts], axis=1)
    tok_weight = token_weights(domain_ids, domain_weights)
    weighted = (tok_weight[:, None] * both.astype(jnp.float32)).astype(jnp.bfloat16)
    pairs = transpose_pairs(n_rows, n_cols, n_dp, n_ring)
    swapped = jnp.concatenate(
        [
            lax.ppermute(out_grads, ROWS + ("feat",), pairs),
            lax.ppermute(acts, ROWS + ("feat",), pairs),
        ],
        axis=1,
    )
    rows = lax.all_gather(swapped, "feat", axis=0, tiled=True)
    cols = gather_columns(weighted, n_dp, n_ring)
    grad_sum = contract_tokens(rows[:, :width_g], cols[:, :width_g])
    act_sum = contract_tokens(rows[:, width_g:], lax.optimization_barrier(cols[:, width_g:]))
    grad_factor = (grad_sum * inv_count).astype(jnp.bfloat16)
    act_factor = (act_sum * inv_count).astype(jnp.bfloat16)
    return (grad_factor, act_factor)


def solution(mesh):
    in_specs = (P(ROWS, "feat"), P(ROWS, "feat"), P(ROWS), P())
    out_specs = (P(ROWS, "feat"), P(ROWS, "feat"))
    return jax.shard_map(local, mesh=mesh, in_specs=in_specs, out_specs=out_specs, check_vma=False)
```

profile of v0, /device:TPU:34, one launch (start us, length us, event | category | flops | bytes accessed | tf_op | source)
XLA Modules:
  0.0 204.5 jit_solution(8906525784769521334)
XLA Ops:
  7.2 0.0 all-gather.2.cloned.1.call-start
  7.2 6.5 %collective-permute-start = (bf16[128,1792]{1,0:T(8,128)(2,1)}, bf16[128,1792]{1,0:T(8,128)(2,1)S(1)}, u32[]{:S(2)}, u32[]{:S(2)}) collective-permute-start(bf16[128,1792]{1,0:T(8,128)(2,1)} %param.4), channel_id=1, source_target_pairs={{0,0},{16,1},{32,2},{48,3},{64,4},{80,5},{96,6},{112,7},{128,8},{1... | collective-permute-start | bytes 1376264 | tf_op jit(solution)/shard_map/ppermute | solution.py:78
  13.7 3.8 %collective-permute-start.1 = (bf16[128,512]{1,0:T(8,128)(2,1)}, bf16[128,512]{1,0:T(8,128)(2,1)S(1)}, u32[]{:S(2)}, u32[]{:S(2)}) collective-permute-start(bf16[128,512]{1,0:T(8,128)(2,1)} %param.5), channel_id=1, source_target_pairs={{0,0},{16,1},{32,2},{48,3},{64,4},{80,5},{96,6},{112,7},{128,8},{1... | collective-permute-start | bytes 393224 | tf_op jit(solution)/shard_map/ppermute | solution.py:79
  17.5 12.0 %collective-permute-done.1 = bf16[128,512]{1,0:T(8,128)(2,1)S(1)} collective-permute-done((bf16[128,512]{1,0:T(8,128)(2,1)}, bf16[128,512]{1,0:T(8,128)(2,1)S(1)}, u32[]{:S(2)}, u32[]{:S(2)}) %collective-permute-start.1) | collective-permute-done | bytes 131104 | tf_op jit(solution)/shard_map/ppermute | solution.py:79
  29.5 0.0 collective-permute-done
  29.5 0.9 pad_maximum_fusion.1
  30.3 0.0 all-gather.2.cloned.1.call-update
  30.4 0.8 select_reduce_fusion
  31.1 1.3 constant_dynamic-update-slice_fusion.5
  32.4 0.1 collective-permute-start.2
  32.5 14.8 %collective-permute-done.2 = bf16[128,2304]{1,0:T(8,128)(2,1)S(1)} collective-permute-done((bf16[128,2304]{1,0:T(8,128)(2,1)S(1)}, bf16[128,2304]{1,0:T(8,128)(2,1)S(1)}, u32[]{:S(2)}, u32[]{:S(2)}) %collective-permute-start.2) | collective-permute-done | bytes 589856 | tf_op jit(solution)/shard_map/ppermute | solution.py:52
  47.3 0.1 pad_maximum_fusion
  47.4 15.8 %collective-permute-start.3 = (bf16[256,2304]{1,0:T(8,128)(2,1)S(1)}, bf16[256,2304]{1,0:T(8,128)(2,1)S(1)}, u32[]{:S(2)}, u32[]{:S(2)}) collective-permute-start(bf16[256,2304]{1,0:T(8,128)(2,1)S(1)} %pad_maximum_fusion), channel_id=1, source_target_pairs={{32,0},{48,16},{64,32},{80,48},{96,64},{112,80},{0,96},{16,112},{3... | collective-permute-start | bytes 3538952 | tf_op jit(solution)/shard_map/ppermute | solution.py:54
  63.2 1.0 collective-permute-start.5
  64.2 23.6 %collective-permute-done.3 = bf16[256,2304]{1,0:T(8,128)(2,1)S(1)} collective-permute-done((bf16[256,2304]{1,0:T(8,128)(2,1)S(1)}, bf16[256,2304]{1,0:T(8,128)(2,1)S(1)}, u32[]{:S(2)}, u32[]{:S(2)}) %collective-permute-start.3) | collective-permute-done | bytes 1179680 | tf_op jit(solution)/shard_map/ppermute | solution.py:54
  87.8 3.7 %collective-permute-start.4 = (bf16[128,2304]{1,0:T(8,128)(2,1)S(1)}, bf16[128,2304]{1,0:T(8,128)(2,1)S(1)}, u32[]{:S(2)}, u32[]{:S(2)}) collective-permute-start(bf16[128,2304]{1,0:T(8,128)(2,1)S(1)} %slice.25), channel_id=1, source_target_pairs={{32,0},{48,16},{64,32},{80,48},{96,64},{112,80},{0,96},{16,112},{3... | collective-permute-start | bytes 1769480 | tf_op jit(solution)/shard_map/ppermute | solution.py:56
  91.5 0.1 constant_dynamic-update-slice_fusion.4
  91.6 0.1 collective-permute-done.5
  91.7 0.6 collective-permute-start.6
  92.4 0.2 constant_dynamic-update-slice_fusion.3
  92.5 12.1 %collective-permute-done.4 = bf16[128,2304]{1,0:T(8,128)(2,1)S(1)} collective-permute-done((bf16[128,2304]{1,0:T(8,128)(2,1)S(1)}, bf16[128,2304]{1,0:T(8,128)(2,1)S(1)}, u32[]{:S(2)}, u32[]{:S(2)}) %collective-permute-start.4) | collective-permute-done | bytes 589856 | tf_op jit(solution)/shard_map/ppermute | solution.py:56
  104.6 0.1 constant_dynamic-update-slice_fusion.2
  104.7 4.2 %collective-permute-done.6 = bf16[128,2304]{1,0:T(8,128)(2,1)S(1)} collective-permute-done((bf16[128,2304]{1,0:T(8,128)(2,1)S(1)}, bf16[128,2304]{1,0:T(8,128)(2,1)S(1)}, u32[]{:S(2)}, u32[]{:S(2)}) %collective-permute-start.6) | collective-permute-done | bytes 589856 | tf_op jit(solution)/shard_map/ppermute | solution.py:57
  108.9 0.1 constant_dynamic-update-slice_fusion.1
  109.0 0.2 constant_dynamic-update-slice_fusion
  109.2 0.8 collective-permute-start.7
  110.0 7.5 %collective-permute-done.7 = bf16[1024,2304]{1,0:T(8,128)(2,1)S(1)} collective-permute-done((bf16[1024,2304]{1,0:T(8,128)(2,1)S(1)}, bf16[1024,2304]{1,0:T(8,128)(2,1)S(1)}, u32[]{:S(2)}, u32[]{:S(2)}) %collective-permute-start.7) | collective-permute-done | bytes 4718624 | tf_op jit(solution)/shard_map/ppermute | solution.py:59
  117.5 0.3 constant_dynamic-update-slice_fusion.6
  117.8 0.0 copy-start
  117.8 3.6 %copy-done = bf16[2048,2304]{1,0:T(8,128)(2,1)} copy-done((bf16[2048,2304]{1,0:T(8,128)(2,1)}, bf16[2048,2304]{1,0:T(8,128)(2,1)S(1)}, u32[]{:S(2)}) %copy-start) | copy-done | bytes 9437208
  121.5 0.2 slice.29
  121.6 52.6 %all-gather.2.cloned.1.call-done = bf16[2048,2304]{1,0:T(8,128)(2,1)} async-done(((bf16[128,2304]{1,0:T(8,128)(2,1)}), bf16[2048,2304]{1,0:T(8,128)(2,1)}) %all-gather.2.cloned.1.call-update) | async-done | bytes 9437200 | tf_op jit(solution)/shard_map/all_gather | solution.py:83
  174.2 19.8 %multiply_convert_fusion = bf16[1792,1792]{1,0:T(8,128)(2,1)} fusion(bf16[2048,2304]{1,0:T(8,128)(2,1)} %copy-done, bf16[2048,2304]{1,0:T(8,128)(2,1)} %all-gather.2.cloned.1.call-done), kind=kOutput, calls=%fused_computation | convolution fusion | flops 13159759872 | bytes 21102592 | tf_op jit(solution)/shard_map/dot_general | solution.py:17
  194.0 3.7 %fusion.7 = bf16[512,512]{1,0:T(8,128)(2,1)} fusion(bf16[2048,512]{1,0:T(8,128)(2,1)S(1)} %slice.29, bf16[2048,2304]{1,0:T(8,128)(2,1)} %all-gather.2.cloned.1.call-done), kind=kOutput, calls=%fused_computation.6 | convolution fusion | flops 1074266112 | bytes 4718592 | tf_op jit(solution)/shard_map/dot_general | solution.py:17
  (4 shorter events, 0.1 us)
Async XLA Ops:
  7.2 167.1 %all-gather.2.cloned.1.call-start = ((), (), s32[]{:S(2)}) async-start(), calls=%async_computation | async-start | bytes 10027008 | tf_op jit(solution)/shard_map/all_gather | solution.py:83
  7.2 22.3 %collective-permute-start = (bf16[128,1792]{1,0:T(8,128)(2,1)}, bf16[128,1792]{1,0:T(8,128)(2,1)S(1)}, u32[]{:S(2)}, u32[]{:S(2)}) collective-permute-start(bf16[128,1792]{1,0:T(8,128)(2,1)} %param.4), channel_id=1, source_target_pairs={{0,0},{16,1},{32,2},{48,3},{64,4},{80,5},{96,6},{112,7},{128,8},{1... | collective-permute-start | bytes 1376264 | tf_op jit(solution)/shard_map/ppermute | solution.py:78
  13.7 15.8 %collective-permute-start.1 = (bf16[128,512]{1,0:T(8,128)(2,1)}, bf16[128,512]{1,0:T(8,128)(2,1)S(1)}, u32[]{:S(2)}, u32[]{:S(2)}) collective-permute-start(bf16[128,512]{1,0:T(8,128)(2,1)} %param.5), channel_id=1, source_target_pairs={{0,0},{16,1},{32,2},{48,3},{64,4},{80,5},{96,6},{112,7},{128,8},{1... | collective-permute-start | bytes 393224 | tf_op jit(solution)/shard_map/ppermute | solution.py:79
  32.4 14.9 %collective-permute-start.2 = (bf16[128,2304]{1,0:T(8,128)(2,1)S(1)}, bf16[128,2304]{1,0:T(8,128)(2,1)S(1)}, u32[]{:S(2)}, u32[]{:S(2)}) collective-permute-start(bf16[128,2304]{1,0:T(8,128)(2,1)S(1)} %get-tuple-element.3), channel_id=1, source_target_pairs={{16,0},{0,16},{48,32},{32,48},{80,64},{64,80},{112,96},{96,112},{1... | collective-permute-start | bytes 1769480 | tf_op jit(solution)/shard_map/ppermute | solution.py:52
  47.4 40.4 %collective-permute-start.3 = (bf16[256,2304]{1,0:T(8,128)(2,1)S(1)}, bf16[256,2304]{1,0:T(8,128)(2,1)S(1)}, u32[]{:S(2)}, u32[]{:S(2)}) collective-permute-start(bf16[256,2304]{1,0:T(8,128)(2,1)S(1)} %pad_maximum_fusion), channel_id=1, source_target_pairs={{32,0},{48,16},{64,32},{80,48},{96,64},{112,80},{0,96},{16,112},{3... | collective-permute-start | bytes 3538952 | tf_op jit(solution)/shard_map/ppermute | solution.py:54
  63.2 28.5 %collective-permute-start.5 = (bf16[256,2304]{1,0:T(8,128)(2,1)S(1)}, bf16[256,2304]{1,0:T(8,128)(2,1)S(1)}, u32[]{:S(2)}, u32[]{:S(2)}) collective-permute-start(bf16[256,2304]{1,0:T(8,128)(2,1)S(1)} %pad_maximum_fusion), channel_id=1, source_target_pairs={{96,0},{112,16},{0,32},{16,48},{32,64},{48,80},{64,96},{80,112},{9... | collective-permute-start | bytes 3538952 | tf_op jit(solution)/shard_map/ppermute | solution.py:55
  87.8 16.8 %collective-permute-start.4 = (bf16[128,2304]{1,0:T(8,128)(2,1)S(1)}, bf16[128,2304]{1,0:T(8,128)(2,1)S(1)}, u32[]{:S(2)}, u32[]{:S(2)}) collective-permute-start(bf16[128,2304]{1,0:T(8,128)(2,1)S(1)} %slice.25), channel_id=1, source_target_pairs={{32,0},{48,16},{64,32},{80,48},{96,64},{112,80},{0,96},{16,112},{3... | collective-permute-start | bytes 1769480 | tf_op jit(solution)/shard_map/ppermute | solution.py:56
  91.7 17.2 %collective-permute-start.6 = (bf16[128,2304]{1,0:T(8,128)(2,1)S(1)}, bf16[128,2304]{1,0:T(8,128)(2,1)S(1)}, u32[]{:S(2)}, u32[]{:S(2)}) collective-permute-start(bf16[128,2304]{1,0:T(8,128)(2,1)S(1)} %slice.26), channel_id=1, source_target_pairs={{96,0},{112,16},{0,32},{16,48},{32,64},{48,80},{64,96},{80,112},{9... | collective-permute-start | bytes 1769480 | tf_op jit(solution)/shard_map/ppermute | solution.py:57
  109.2 8.3 %collective-permute-start.7 = (bf16[1024,2304]{1,0:T(8,128)(2,1)S(1)}, bf16[1024,2304]{1,0:T(8,128)(2,1)S(1)}, u32[]{:S(2)}, u32[]{:S(2)}) collective-permute-start(bf16[1024,2304]{1,0:T(8,128)(2,1)S(1)} %get-tuple-element.4), channel_id=1, source_target_pairs={{128,0},{0,128},{129,1},{1,129},{130,2},{2,130},{131,3},{3,131},{1... | collective-permute-start | bytes 14155784 | tf_op jit(solution)/shard_map/ppermute | solution.py:59
  117.8 3.7 %copy-start = (bf16[2048,2304]{1,0:T(8,128)(2,1)}, bf16[2048,2304]{1,0:T(8,128)(2,1)S(1)}, u32[]{:S(2)}) copy-start(bf16[2048,2304]{1,0:T(8,128)(2,1)S(1)} %constant_dynamic-update-slice_fusion.6) | copy-start | bytes 28311556
Sparse Core Ops, SparseCore 0:
  30.5 143.6 all-gather.1
where the time goes:
time: 205 us
  waiting for transfers between devices  127 us (62%)
  starting transfers between devices  32.2 us (16%)
  matrix products  23.5 us (11%)
  between operations  14.1 us (7%)
  local copies, waits for them, and re-layouts  4.76 us (2%)
  other arithmetic  2.95 us (1%)
    all_gather x1, waiting for transfers between devices, local(): rows = lax.all_gather(swapped, 'feat', axis=0, tiled=True)  52.6 us
    ppermute x1, waiting for transfers between devices, gather_columns(): ahead = lax.ppermute(own, 'ctx', ctx_shift(n_ring, 1, 0))  23.6 us
    dot_general x2, matrix products, contract_tokens(): lax.dot_general(left, right, (((0,), (0,)), ((), ())), preferred_element_...  23.5 us
    ppermute x1, starting transfers between devices, gather_columns(): ahead = lax.ppermute(own, 'ctx', ctx_shift(n_ring, 1, 0))  15.8 us
    ppermute x1, waiting for transfers between devices, gather_columns(): near = lax.ppermute(block, 'ctx', ctx_shift(n_ring, 0, 1))  14.8 us
    ppermute x1, waiting for transfers between devices, gather_columns(): far_a = lax.ppermute(ahead[:half], 'ctx', ctx_shift(n_ring, 1, 0))  12.1 us
    ppermute x1, waiting for transfers between devices, local(): lax.ppermute(acts, ROWS + ('feat',), pairs)  12 us
    ppermute x1, waiting for transfers between devices, gather_columns(): other = lax.ppermute(mine, 'dp', [(1, 0), (0, 1)])  7.54 us
  transfers between devices with their start and end apart: 9, of which 8 were waited for; matrix products, arithmetic and copies ran while one was open for 2% of the time, Pallas kernels for 0%

commit v1 on v0

--- a/solution.py
+++ b/solution.py
@@ -80,7 +80,14 @@
         ],
         axis=1,
     )
-    rows = lax.all_gather(swapped, "feat", axis=0, tiled=True)
+
+    def _connect_roads(u_in):
+        d_next = lax.psum(1, "feat")
+        latest = jnp.stack(d_next * [u_in], 0)
+        out_arr = lax.all_to_all(latest, "feat", 0, 0)
+        return jnp.concatenate(out_arr, axis=0)
+
+    rows = _connect_roads(swapped)
     cols = gather_columns(weighted, n_dp, n_ring)
     grad_sum = contract_tokens(rows[:, :width_g], cols[:, :width_g])
     act_sum = contract_tokens(rows[:, width_g:], lax.optimization_barrier(cols[:, width_g:]))

time: 205 us -> 381 us (1.86)
  the two profiles are of different devices: /device:TPU:34 before, /device:TPU:195 now
where the time goes in v1:
time: 381 us
  waiting for transfers between devices  324 us (85%)
  matrix products  23.6 us (6%)
  starting transfers between devices  22.4 us (6%)
  local copies, waits for them, and re-layouts  9.4 us (2%)
    ppermute x1, waiting for transfers between devices, gather_columns(): near = lax.ppermute(block, 'ctx', ctx_shift(n_ring, 0, 1))  250 us
    ppermute x1, waiting for transfers between devices, local(): lax.ppermute(acts, ROWS + ('feat',), pairs)  27 us
    ppermute x1, waiting for transfers between devices, gather_columns(): ahead = lax.ppermute(own, 'ctx', ctx_shift(n_ring, 1, 0))  25.4 us
    dot_general x2, matrix products, contract_tokens(): lax.dot_general(left, right, (((0,), (0,)), ((), ())), preferred_element_...  23.6 us
    ppermute x1, waiting for transfers between devices, gather_columns(): far_a = lax.ppermute(ahead[:half], 'ctx', ctx_shift(n_ring, 1, 0))  11.4 us
  transfers between devices with their start and end apart: 9, of which 6 were waited for; matrix products, arithmetic and copies ran while one was open for 0% of the time, Pallas kernels for 0%

profile of v1, /device:TPU:195, one launch (start us, length us, event | category | flops | bytes accessed | tf_op | source)
XLA Modules:
  0.0 380.8 jit_solution(12577616481432010250)
XLA Ops:
  0.6 6.6 %collective-permute-start = (bf16[128,1792]{1,0:T(8,128)(2,1)}, bf16[128,1792]{1,0:T(8,128)(2,1)S(1)}, u32[]{:S(2)}, u32[]{:S(2)}) collective-permute-start(bf16[128,1792]{1,0:T(8,128)(2,1)} %param.4), channel_id=1, source_target_pairs={{0,0},{16,1},{32,2},{48,3},{64,4},{80,5},{96,6},{112,7},{128,8},{1... | collective-permute-start | bytes 1376264 | tf_op jit(solution)/shard_map/ppermute | solution.py:78
  7.2 1.9 collective-permute-start.1
  9.2 27.0 %collective-permute-done.1 = bf16[128,512]{1,0:T(8,128)(2,1)S(1)} collective-permute-done((bf16[128,512]{1,0:T(8,128)(2,1)}, bf16[128,512]{1,0:T(8,128)(2,1)S(1)}, u32[]{:S(2)}, u32[]{:S(2)}) %collective-permute-start.1) | collective-permute-done | bytes 131104 | tf_op jit(solution)/shard_map/ppermute | solution.py:79
  36.2 0.0 collective-permute-done
  36.2 4.6 %stack.2 = bf16[16,128,2304]{2,1,0:T(8,128)(2,1)} broadcast(bf16[128,2304]{1,0:T(8,128)(2,1)S(1)} %pad_maximum_fusion.1), dimensions={1,2} | broadcast | bytes 10027008 | tf_op jit(solution)/shard_map/stack | solution.py:86
  40.8 0.0 copy-start.3
  40.8 0.0 copy-start.4
  40.8 0.0 copy-start.1
  40.8 0.0 copy-start.2
  40.8 7.1 %all-to-all-start = ((bf16[16,128,2304]{2,1,0:T(8,128)(2,1)}), bf16[16,128,2304]{2,1,0:T(8,128)(2,1)}, u32[]{:S(2)}, u32[]{:S(2)}) async-start(bf16[16,128,2304]{2,1,0:T(8,128)(2,1)} %stack.2), calls=%async_computation | async-start | bytes 18874368 | tf_op jit(solution)/shard_map/all_to_all | solution.py:87
  47.9 0.0 copy-done.3
  47.9 0.0 copy-done.4
  47.9 0.1 select_reduce_fusion
  48.0 0.0 copy-done.1
  48.0 0.0 copy-done.2
  48.0 0.2 constant_dynamic-update-slice_fusion.5
  48.2 0.9 collective-permute-start.2
  49.1 250.0 %collective-permute-done.2 = bf16[128,2304]{1,0:T(8,128)(2,1)S(1)} collective-permute-done((bf16[128,2304]{1,0:T(8,128)(2,1)S(1)}, bf16[128,2304]{1,0:T(8,128)(2,1)S(1)}, u32[]{:S(2)}, u32[]{:S(2)}) %collective-permute-start.2) | collective-permute-done | bytes 589856 | tf_op jit(solution)/shard_map/ppermute | solution.py:52
  299.2 0.1 pad_maximum_fusion
  299.2 0.1 collective-permute-start.3
  299.3 1.5 collective-permute-start.5
  300.8 25.4 %collective-permute-done.3 = bf16[256,2304]{1,0:T(8,128)(2,1)S(1)} collective-permute-done((bf16[256,2304]{1,0:T(8,128)(2,1)S(1)}, bf16[256,2304]{1,0:T(8,128)(2,1)S(1)}, u32[]{:S(2)}, u32[]{:S(2)}) %collective-permute-start.3) | collective-permute-done | bytes 1179680 | tf_op jit(solution)/shard_map/ppermute | solution.py:54
  326.2 1.6 collective-permute-start.4
  327.9 0.1 constant_dynamic-update-slice_fusion.4
  327.9 0.0 collective-permute-done.5
  328.0 0.1 collective-permute-start.6
  328.1 0.2 constant_dynamic-update-slice_fusion.3
  328.3 11.4 %collective-permute-done.4 = bf16[128,2304]{1,0:T(8,128)(2,1)S(1)} collective-permute-done((bf16[128,2304]{1,0:T(8,128)(2,1)S(1)}, bf16[128,2304]{1,0:T(8,128)(2,1)S(1)}, u32[]{:S(2)}, u32[]{:S(2)}) %collective-permute-start.4) | collective-permute-done | bytes 589856 | tf_op jit(solution)/shard_map/ppermute | solution.py:56
  339.7 0.1 constant_dynamic-update-slice_fusion.2
  339.7 2.9 collective-permute-done.6
  342.7 0.1 constant_dynamic-update-slice_fusion.1
  342.8 0.2 constant_dynamic-update-slice_fusion
  342.9 2.6 collective-permute-start.7
  345.5 7.5 %collective-permute-done.7 = bf16[1024,2304]{1,0:T(8,128)(2,1)S(1)} collective-permute-done((bf16[1024,2304]{1,0:T(8,128)(2,1)S(1)}, bf16[1024,2304]{1,0:T(8,128)(2,1)S(1)}, u32[]{:S(2)}, u32[]{:S(2)}) %collective-permute-start.7) | collective-permute-done | bytes 4718624 | tf_op jit(solution)/shard_map/ppermute | solution.py:59
  353.1 0.3 constant_dynamic-update-slice_fusion.6
  353.4 0.0 copy-start
  353.4 3.7 copy-done
  357.1 0.2 slice.29
  357.3 0.0 all-to-all-done
  357.3 19.9 %multiply_convert_fusion = bf16[1792,1792]{1,0:T(8,128)(2,1)} fusion(bf16[2048,2304]{1,0:T(8,128)(2,1)} %copy-done, bf16[2048,2304]{1,0:T(8,128)(2,1)} %bitcast), kind=kOutput, calls=%fused_computation | convolution fusion | flops 13159759872 | bytes 21102592 | tf_op jit(solution)/shard_map/dot_general | solution.py:17
  377.2 3.7 fusion.7
  (5 shorter events, 0.2 us)
Async XLA Ops:
  0.6 35.5 %collective-permute-start = (bf16[128,1792]{1,0:T(8,128)(2,1)}, bf16[128,1792]{1,0:T(8,128)(2,1)S(1)}, u32[]{:S(2)}, u32[]{:S(2)}) collective-permute-start(bf16[128,1792]{1,0:T(8,128)(2,1)} %param.4), channel_id=1, source_target_pairs={{0,0},{16,1},{32,2},{48,3},{64,4},{80,5},{96,6},{112,7},{128,8},{1... | collective-permute-start | bytes 1376264 | tf_op jit(solution)/shard_map/ppermute | solution.py:78
  7.2 28.9 %collective-permute-start.1 = (bf16[128,512]{1,0:T(8,128)(2,1)}, bf16[128,512]{1,0:T(8,128)(2,1)S(1)}, u32[]{:S(2)}, u32[]{:S(2)}) collective-permute-start(bf16[128,512]{1,0:T(8,128)(2,1)} %param.5), channel_id=1, source_target_pairs={{0,0},{16,1},{32,2},{48,3},{64,4},{80,5},{96,6},{112,7},{128,8},{1... | collective-permute-start | bytes 393224 | tf_op jit(solution)/shard_map/ppermute | solution.py:79
  40.8 7.1 %copy-start.3 = (s32[8]{0:T(128)S(1)}, s32[8]{0:T(128)}, u32[]{:S(2)}) copy-start(s32[8]{0:T(128)} %param.7) | copy-start | bytes 100
  40.8 7.1 %copy-start.4 = (s32[128]{0:T(128)S(1)}, s32[128]{0:T(128)}, u32[]{:S(2)}) copy-start(s32[128]{0:T(128)} %param.6) | copy-start | bytes 1540
  40.8 7.2 %copy-start.1 = (bf16[128,1792]{1,0:T(8,128)(2,1)S(1)}, bf16[128,1792]{1,0:T(8,128)(2,1)}, u32[]{:S(2)}) copy-start(bf16[128,1792]{1,0:T(8,128)(2,1)} %param.4) | copy-start | bytes 1376260
  40.8 7.2 %copy-start.2 = (bf16[128,512]{1,0:T(8,128)(2,1)S(1)}, bf16[128,512]{1,0:T(8,128)(2,1)}, u32[]{:S(2)}) copy-start(bf16[128,512]{1,0:T(8,128)(2,1)} %param.5) | copy-start | bytes 393220
  40.8 316.5 %all-to-all-start = ((bf16[16,128,2304]{2,1,0:T(8,128)(2,1)}), bf16[16,128,2304]{2,1,0:T(8,128)(2,1)}, u32[]{:S(2)}, u32[]{:S(2)}) async-start(bf16[16,128,2304]{2,1,0:T(8,128)(2,1)} %stack.2), calls=%async_computation | async-start | bytes 18874368 | tf_op jit(solution)/shard_map/all_to_all | solution.py:87
  48.2 251.0 %collective-permute-start.2 = (bf16[128,2304]{1,0:T(8,128)(2,1)S(1)}, bf16[128,2304]{1,0:T(8,128)(2,1)S(1)}, u32[]{:S(2)}, u32[]{:S(2)}) collective-permute-start(bf16[128,2304]{1,0:T(8,128)(2,1)S(1)} %get-tuple-element.3), channel_id=1, source_target_pairs={{16,0},{0,16},{48,32},{32,48},{80,64},{64,80},{112,96},{96,112},{1... | collective-permute-start | bytes 1769480 | tf_op jit(solution)/shard_map/ppermute | solution.py:52
  299.2 27.0 %collective-permute-start.3 = (bf16[256,2304]{1,0:T(8,128)(2,1)S(1)}, bf16[256,2304]{1,0:T(8,128)(2,1)S(1)}, u32[]{:S(2)}, u32[]{:S(2)}) collective-permute-start(bf16[256,2304]{1,0:T(8,128)(2,1)S(1)} %pad_maximum_fusion), channel_id=1, source_target_pairs={{32,0},{48,16},{64,32},{80,48},{96,64},{112,80},{0,96},{16,112},{3... | collective-permute-start | bytes 3538952 | tf_op jit(solution)/shard_map/ppermute | solution.py:54
  299.3 28.6 %collective-permute-start.5 = (bf16[256,2304]{1,0:T(8,128)(2,1)S(1)}, bf16[256,2304]{1,0:T(8,128)(2,1)S(1)}, u32[]{:S(2)}, u32[]{:S(2)}) collective-permute-start(bf16[256,2304]{1,0:T(8,128)(2,1)S(1)} %pad_maximum_fusion), channel_id=1, source_target_pairs={{96,0},{112,16},{0,32},{16,48},{32,64},{48,80},{64,96},{80,112},{9... | collective-permute-start | bytes 3538952 | tf_op jit(solution)/shard_map/ppermute | solution.py:55
  326.2 13.4 %collective-permute-start.4 = (bf16[128,2304]{1,0:T(8,128)(2,1)S(1)}, bf16[128,2304]{1,0:T(8,128)(2,1)S(1)}, u32[]{:S(2)}, u32[]{:S(2)}) collective-permute-start(bf16[128,2304]{1,0:T(8,128)(2,1)S(1)} %slice.25), channel_id=1, source_target_pairs={{32,0},{48,16},{64,32},{80,48},{96,64},{112,80},{0,96},{16,112},{3... | collective-permute-start | bytes 1769480 | tf_op jit(solution)/shard_map/ppermute | solution.py:56
  328.0 14.7 %collective-permute-start.6 = (bf16[128,2304]{1,0:T(8,128)(2,1)S(1)}, bf16[128,2304]{1,0:T(8,128)(2,1)S(1)}, u32[]{:S(2)}, u32[]{:S(2)}) collective-permute-start(bf16[128,2304]{1,0:T(8,128)(2,1)S(1)} %slice.26), channel_id=1, source_target_pairs={{96,0},{112,16},{0,32},{16,48},{32,64},{48,80},{64,96},{80,112},{9... | collective-permute-start | bytes 1769480 | tf_op jit(solution)/shard_map/ppermute | solution.py:57
  342.9 10.2 %collective-permute-start.7 = (bf16[1024,2304]{1,0:T(8,128)(2,1)S(1)}, bf16[1024,2304]{1,0:T(8,128)(2,1)S(1)}, u32[]{:S(2)}, u32[]{:S(2)}) collective-permute-start(bf16[1024,2304]{1,0:T(8,128)(2,1)S(1)} %get-tuple-element.4), channel_id=1, source_target_pairs={{128,0},{0,128},{129,1},{1,129},{130,2},{2,130},{131,3},{3,131},{1... | collective-permute-start | bytes 14155784 | tf_op jit(solution)/shard_map/ppermute | solution.py:59
  353.4 3.7 copy-start
